TPU v7x, 256 devices: a whole 4x4x8 slice. The times are simulated.
256 devices in a mesh: row: 8 (over y, core), col: 32 (over z, x).
Axes of the slice: x: 4, y: 4, z: 8, core: 2. Of those that a mesh axis runs over, the one named last changes fastest.
Arguments:
- blocks: float32 [128, 32, 256, 256], P('row', 'col'), may hold values from -6 to 6
- panel_rows: int32 [2, 64], P(None, 'row'), may hold values from -1 to 767, as said below
- target_slots: int32 [2, 128, 32], P(None, 'row', 'col'), may hold values from -1 to 7, as said below
- diag_inverse: float32 [2, 256, 256], replicated, may hold values from -1 to 1, as said below
- cross_block: float32 [256, 256], replicated, may hold values from -6 to 6
Outputs:
- factored: float32 [128, 32, 256, 256], P('row', 'col')
Inputs may be any that keep to these rules, and one draw needn't show every extreme that they name: `panel_rows`: slot q * 2 + m of row device r stands for the m-th structure row of block column class r + q times the number of row devices; both lists are -1 where that class is 0 or 1, and list 0 is -1 also where block column 0 lacks the row; otherwise list 0 equals list 1. `target_slots`: A filled slot of class c names in entry 0 a slot of its own row device and in entry 1 a slot of row device c modulo the number of row devices, within (c // number of row devices) * 2 and the 1 after it; both are filled or both -1, always -1 in classes 0 and 1; the target's block row number is at least its block column number. `diag_inverse`: each matrix is lower triangular.
All inputs are finite; a program needn't handle non-finite values.
Results may differ from a plain program's by a relative error of at most 0.0003.
Values sent between devices are 32-bit elements; how exact they have to be, the bound alone decides.
No kernel may reach another device: no remote copies, remote signals or barrier semaphores. Data moves between devices by JAX's collectives and lax.ppermute only.
A program may use at most 128 MiB of HBM per device.

v0:
```python
import jax
import jax.numpy as jnp
from jax import lax
from jax.sharding import PartitionSpec as P

PER_CLASS = 2
HIGHEST_PRECISION = lax.Precision.HIGHEST


def broadcast(array, axis, root):
    mine = lax.axis_index(axis) == root
    return lax.psum(jnp.where(mine, array, jnp.zeros_like(array)), axis)


def apply_inverse(panel_rows_block, inverse):
    return jnp.einsum("ab,cb->ac", panel_rows_block, inverse, precision=HIGHEST_PRECISION)


def per_device(blocks, panel_rows, target_slots, diag_inverse, cross_block):
    column = lax.axis_index("col")
    row_count = lax.axis_size("row")
    col_count = lax.axis_size("col")
    stored = blocks[:, 0]
    slot_count = panel_rows.shape[1]
    block = stored.shape[-1]
    head_part = stored[:slot_count]
    chunk = slot_count * block // col_count
    pieces = head_part.reshape(col_count, chunk, block)
    received = lax.all_to_all(pieces, "col", 0, 0, tiled=True)
    zero_rows = received[0]
    one_rows = received[1]
    piece_slot = column * chunk // block
    first_live = lax.dynamic_index_in_dim(panel_rows[0], piece_slot, keepdims=False) >= 0
    second_live = lax.dynamic_index_in_dim(panel_rows[1], piece_slot, keepdims=False) >= 0
    cross_factor = jnp.dot(cross_block, diag_inverse[0].T, precision=HIGHEST_PRECISION)
    first_piece = jnp.where(first_live, apply_inverse(zero_rows, diag_inverse[0]), 0.0)
    updated_piece = one_rows - apply_inverse(first_piece, cross_factor)
    second_piece = jnp.where(second_live, apply_inverse(updated_piece, diag_inverse[1]), 0.0)
    both_pieces = jnp.stack([first_piece, second_piece])
    both_rows = lax.all_gather(both_pieces, "col", axis=1, tiled=True)
    both_rows = both_rows.reshape(2, slot_count, block, block)
    first_rows = both_rows[0]
    second_rows = both_rows[1]
    class_start = column // row_count * PER_CLASS
    owner_row = column % row_count
    both_cols = broadcast(
        lax.dynamic_slice_in_dim(both_rows, class_start, PER_CLASS, 1), "row", owner_row
    )
    first_cols = both_cols[0]
    second_cols = both_cols[1]
    row_index = target_slots[0, :, 0]
    col_index = target_slots[1, :, 0]
    present = row_index >= 0
    left_slot = jnp.where(present, row_index, 0)
    right_slot = jnp.where(present, col_index - class_start, 0)
    left_blocks = jnp.concatenate([first_rows[left_slot], second_rows[left_slot]], axis=2)
    right_blocks = jnp.concatenate([first_cols[right_slot], second_cols[right_slot]], axis=2)
    schur_term = jnp.einsum("sak,sbk->sab", left_blocks, right_blocks, precision=HIGHEST_PRECISION)
    trailing = stored - jnp.where(present[:, None, None], schur_term, 0.0)
    head_live = panel_rows >= 0
    keep_mask = ((column == 0) & head_live[0] | (column == 1) & head_live[1])[:, None, None]
    own_panel = jnp.where(column == 0, first_rows, second_rows)
    head_blocks = jnp.where(keep_mask, own_panel, trailing[:slot_count])
    factored = jnp.concatenate([head_blocks, trailing[slot_count:]], axis=0)
    return factored[:, None]


def solution(mesh):
    return jax.shard_map(
        per_device,
        mesh=mesh,
        in_specs=(P("row", "col", None, None), P(None, "row"), P(None, "row", "col"), P(), P()),
        out_specs=P("row", "col", None, None),
        check_vma=False,
    )
```

profile of v0, /device:TPU:2, one launch (start us, length us, event | category | flops | bytes accessed | tf_op | source)
XLA Modules:
  0.0 260.4 jit_solution(12338296099703063530)
XLA Ops:
  6.5 0.0 copy-start
  6.5 0.0 copy-start.4
  6.5 0.0 copy-start.2
  6.5 3.1 %slice.58 = f32[8,1,256,256]{3,2,1,0:T(8,128)} slice(f32[16,1,256,256]{3,2,1,0:T(8,128)} %param.5), slice={[0:8], [0:1], [0:256], [0:256]} | slice | bytes 4194304 | tf_op jit(solution)/shard_map/slice | solution.py:26
  9.7 0.0 copy-start.3
  9.7 11.7 %all-to-all-start = ((f32[32,64,256]{2,1,0:T(8,128)}), f32[32,64,256]{2,1,0:T(8,128)S(1)}, u32[]{:S(2)}, u32[]{:S(2)}) async-start(f32[32,64,256]{2,1,0:T(8,128)} %bitcast.2), calls=%async_computation | async-start | bytes 4194304 | tf_op jit(solution)/shard_map/all_to_all | solution.py:29
  21.4 0.0 all-gather.2.cloned.1.call-start
  21.5 0.0 copy-done.4
  21.5 0.7 fusion.24
  22.2 0.0 copy-done
  22.2 0.0 copy-done.2
  22.2 0.4 fusion.13
  22.6 48.0 %all-to-all-done = f32[32,64,256]{2,1,0:T(8,128)S(1)} async-done(((f32[32,64,256]{2,1,0:T(8,128)}), f32[32,64,256]{2,1,0:T(8,128)S(1)}, u32[]{:S(2)}, u32[]{:S(2)}) %all-to-all-start) | async-done | bytes 2097184 | tf_op jit(solution)/shard_map/all_to_all | solution.py:29
  70.7 0.9 convolution_select_fusion.1
  71.6 0.4 convolution_subtract_fusion
  71.9 1.1 fusion.7
  73.0 0.7 pad_maximum_fusion
  73.7 0.0 all-gather.2.cloned.1.call-update
  73.7 0.0 all-reduce.2.cloned.1.call-start
  73.8 0.0 copy-done.3
  73.9 78.7 %all-gather.2.cloned.1.call-done = f32[2,2048,256]{2,1,0:T(8,128)} async-done(((f32[2,64,256]{2,1,0:T(8,128)}), f32[2,2048,256]{2,1,0:T(8,128)}) %all-gather.2.cloned.1.call-update) | async-done | bytes 4194320 | tf_op jit(solution)/shard_map/all_gather | solution.py:40
  152.5 2.3 dynamic-slice_select_fusion
  154.8 0.0 all-reduce.2.cloned.1.call-update
  154.8 3.8 %fusion.22 = (f32[1,2048,256]{2,1,0:T(8,128)S(1)}, f32[1,2048,256]{2,1,0:T(8,128)}) fusion(f32[2,2048,256]{2,1,0:T(8,128)} %all-gather.2.cloned.1.call-done), kind=kLoop, calls=%fused_computation.45 | loop fusion | bytes 8388608 | tf_op jit(solution)/shard_map/slice | solution.py:42
  158.7 2.8 %gather_fusion = f32[16,256,256]{2,1,0:T(8,128)} fusion(f32[8,256,256]{2,1,0:T(8,128)S(1)} %bitcast.55, s32[1024]{0:T(1024)S(1)} %get-tuple-element.18), kind=kCustom, calls=%fused_computation | custom fusion | bytes 8388672 | tf_op jit(solution)/shard_map/gather | solution.py:56
  161.5 4.4 %gather_fusion.1 = f32[16,256,256]{2,1,0:T(8,128)} fusion(f32[8,256,256]{2,1,0:T(8,128)} %bitcast.57, s32[1024]{0:T(1024)S(1)} %get-tuple-element.18), kind=kCustom, calls=%fused_computation.1 | custom fusion | bytes 8388672 | tf_op jit(solution)/shard_map/gather | solution.py:56
  165.8 55.4 %all-reduce.2.cloned.1.call-done = f32[2,2,256,256]{3,2,1,0:T(8,128)} async-done(((f32[2,2,256,256]{3,2,1,0:T(8,128)}), f32[2,2,256,256]{3,2,1,0:T(8,128)}) %all-reduce.2.cloned.1.call-update) | async-done | bytes 1048592 | tf_op jit(solution)/shard_map/psum | solution.py:12
  221.2 1.3 slice_bitcast_fusion.1
  222.5 2.8 %gather_fusion.2 = f32[16,256,256]{2,1,0:T(8,128)} fusion(f32[2,256,256]{2,1,0:T(8,128)S(1)} %get-tuple-element.9, s32[1024]{0:T(1024)S(1)} %get-tuple-element.17), kind=kCustom, calls=%fused_computation.2 | custom fusion | bytes 8388672 | tf_op jit(solution)/shard_map/gather | solution.py:57
  225.2 2.8 %gather_fusion.3 = f32[16,256,256]{2,1,0:T(8,128)} fusion(f32[2,256,256]{2,1,0:T(8,128)S(1)} %get-tuple-element.10, s32[1024]{0:T(1024)S(1)} %get-tuple-element.17), kind=kCustom, calls=%fused_computation.3 | custom fusion | bytes 8388672 | tf_op jit(solution)/shard_map/gather | solution.py:57
  228.1 0.0 copy-start.1
  228.1 22.4 %bitcast_subtract_fusion = f32[16,256,256]{2,1,0:T(8,128)S(1)} fusion(f32[16,1,256,256]{3,2,1,0:T(8,128)} %param.5, pred[16]{0:T(512)(128)(4,1)S(1)} %compare_bitcast_fusion, f32[16,256,256]{2,1,0:T(8,128)} %gather_fusion.3, f32[16,256,256]{2,1,0:T(8,128)} %gather_fusion.2, f32[16,256,256]{2,1,0:T(8,128)} %gather_fusion.1, f32[16,256,256]{2,1,0:T(8,128)} %gather_fusion), kind=kOutput, calls=%fused_computation.12 | convolution fusion | flops 6448742400 | bytes 25165840 | tf_op jit(solution)/shard_map/sak,sbk->sab/dot_general | solution.py:58
  250.5 0.0 copy-done.1
  250.5 0.6 slice_select_fusion
  251.1 2.4 maximum_bitcast_fusion
  (6 shorter events, 0.0 us)
Async XLA Ops:
  6.5 15.6 %copy-start = (f32[256,256]{1,0:T(8,128)S(1)}, f32[256,256]{1,0:T(8,128)}, u32[]{:S(2)}) copy-start(f32[256,256]{1,0:T(8,128)} %param.9) | copy-start | bytes 786436
  6.5 14.9 %copy-start.4 = (s32[2,8]{1,0:T(2,128)S(1)}, s32[2,8]{1,0:T(2,128)}, u32[]{:S(2)}) copy-start(s32[2,8]{1,0:T(2,128)} %param.6) | copy-start | bytes 196
  6.5 15.6 %copy-start.2 = (f32[2,256,256]{2,1,0:T(8,128)S(1)}, f32[2,256,256]{2,1,0:T(8,128)}, u32[]{:S(2)}) copy-start(f32[2,256,256]{2,1,0:T(8,128)} %param.8) | copy-start | bytes 1572868
  9.7 64.1 %copy-start.3 = (s32[2,16,1]{1,2,0:T(1,128)S(1)}, s32[2,16,1]{1,2,0:T(1,128)}, u32[]{:S(2)}) copy-start(s32[2,16,1]{1,2,0:T(1,128)} %param.7) | copy-start | bytes 388
  9.7 61.0 %all-to-all-start = ((f32[32,64,256]{2,1,0:T(8,128)}), f32[32,64,256]{2,1,0:T(8,128)S(1)}, u32[]{:S(2)}, u32[]{:S(2)}) async-start(f32[32,64,256]{2,1,0:T(8,128)} %bitcast.2), calls=%async_computation | async-start | bytes 4194304 | tf_op jit(solution)/shard_map/all_to_all | solution.py:29
  21.4 131.1 %all-gather.2.cloned.1.call-start = ((), (), s32[]{:S(2)}) async-start(), calls=%async_computation.1 | async-start | bytes 4325376 | tf_op jit(solution)/shard_map/all_gather | solution.py:40
  73.7 147.5 %all-reduce.2.cloned.1.call-start = ((), (), s32[]{:S(2)}) async-start(), calls=%async_computation.2 | async-start | bytes 2097152 | tf_op jit(solution)/shard_map/psum | solution.py:12
  228.1 22.5 %copy-start.1 = (f32[1,2048,256]{2,1,0:T(8,128)S(1)}, f32[1,2048,256]{2,1,0:T(8,128)}, u32[]{:S(2)}) copy-start(f32[1,2048,256]{2,1,0:T(8,128)} %get-tuple-element.8) | copy-start | bytes 6291460
Sparse Core Ops, SparseCore 0:
  73.8 78.6 all-gather.1
  154.9 66.1 all-reduce.1
where the time goes:
time: 261 us; the launch traced here: 260 us
  waiting for transfers between devices  182 us (70%)
  matrix products  25.2 us (10%)
  local copies, waits for them, and re-layouts  21 us (8%)
  between operations  13.6 us (5%)
  starting transfers between devices  11.8 us (5%)
  other arithmetic  6.69 us (3%)
    all_gather x1, waiting for transfers between devices, per_device(): both_rows = lax.all_gather(both_pieces, 'col', axis=1, tiled=True)  78.7 us
    psum x1, waiting for transfers between devices, broadcast(): return lax.psum(jnp.where(mine, array, jnp.zeros_like(array)), axis)  55.4 us
    all_to_all x1, waiting for transfers between devices, per_device(): received = lax.all_to_all(pieces, 'col', 0, 0, tiled=True)  48 us
    dot_general x1, matrix products, per_device(): jnp.einsum('sak,sbk->sab', left_blocks, right_blocks, precision=HIGHEST_P...  22.4 us
    all_to_all x1, starting transfers between devices, per_device(): received = lax.all_to_all(pieces, 'col', 0, 0, tiled=True)  11.7 us
  transfers between devices with their start and end apart: 3, of which 3 were waited for; matrix products, arithmetic and copies ran while one was open for 5% of the time, Pallas kernels for 0%

commit v1 on v0

--- a/solution.py
+++ b/solution.py
@@ -5,6 +5,13 @@
 
 PER_CLASS = 2
 HIGHEST_PRECISION = lax.Precision.HIGHEST
+
+
+def all_by_exchange(shard, axis, d):
+    size = lax.axis_size(axis)
+    pieces = jnp.stack([shard for _ in range(size)])
+    pieces = lax.all_to_all(pieces, axis, split_axis=0, concat_axis=0)
+    return jnp.concatenate(pieces, axis=d)
 
 
 def broadcast(array, axis, root):
@@ -37,7 +44,7 @@
     updated_piece = one_rows - apply_inverse(first_piece, cross_factor)
     second_piece = jnp.where(second_live, apply_inverse(updated_piece, diag_inverse[1]), 0.0)
     both_pieces = jnp.stack([first_piece, second_piece])
-    both_rows = lax.all_gather(both_pieces, "col", axis=1, tiled=True)
+    both_rows = all_by_exchange(both_pieces, "col", 1)
     both_rows = both_rows.reshape(2, slot_count, block, block)
     first_rows = both_rows[0]
     second_rows = both_rows[1]

time: 261 us -> 287 us (1.100)
  waiting for transfers between devices: 182 us -> 196 us
  local copies, waits for them, and re-layouts: 21 us -> 28.2 us
  starting transfers between devices: 11.8 us -> 18.9 us
    all_to_all x0 -> x1, waiting for transfers between devices: none -> 91.5 us  [all_by_exchange(): pieces = lax.all_to_all(pieces, axis, split_axis=0, concat_axis=0)]
    all_gather x1 -> x0, waiting for transfers between devices: 78.7 us -> none  [per_device(): both_rows = lax.all_gather(both_pieces, 'col', axis=1, tiled=True)]
    all_to_all x0 -> x1, starting transfers between devices: none -> 7.05 us  [all_by_exchange(): pieces = lax.all_to_all(pieces, axis, split_axis=0, concat_axis=0)]
  transfers between devices with their start and end apart: 3 -> 3, of which waited for: 3 -> 3; matrix products, arithmetic and copies ran while one was open for 5% -> 4% of each run, Pallas kernels for 0% -> 0%
where the time goes in v1:
time: 287 us
  waiting for transfers between devices  196 us (68%)
  local copies, waits for them, and re-layouts  28.2 us (10%)
  matrix products  25.2 us (9%)
  starting transfers between devices  18.9 us (7%)
  between operations  13.6 us (5%)
  other arithmetic  4.81 us (2%)
    all_to_all x1, waiting for transfers between devices, all_by_exchange(): pieces = lax.all_to_all(pieces, axis, split_axis=0, concat_axis=0)  91.5 us
    psum x1, waiting for transfers between devices, broadcast(): return lax.psum(jnp.where(mine, array, jnp.zeros_like(array)), axis)  56.5 us
    all_to_all x1, waiting for transfers between devices, per_device(): received = lax.all_to_all(pieces, 'col', 0, 0, tiled=True)  48.1 us
    dot_general x1, matrix products, per_device(): jnp.einsum('sak,sbk->sab', left_blocks, right_blocks, precision=HIGHEST_P...  22.4 us
    all_to_all x1, starting transfers between devices, per_device(): received = lax.all_to_all(pieces, 'col', 0, 0, tiled=True)  11.6 us
    all_to_all x1, starting transfers between devices, all_by_exchange(): pieces = lax.all_to_all(pieces, axis, split_axis=0, concat_axis=0)  7.05 us
  transfers between devices with their start and end apart: 3, of which 3 were waited for; matrix products, arithmetic and copies ran while one was open for 4% of the time, Pallas kernels for 0%

profile of v1, /device:TPU:2, one launch (start us, length us, event | category | flops | bytes accessed | tf_op | source)
XLA Modules:
  0.0 286.8 jit_solution(13020527015502377754)
XLA Ops:
  6.5 0.0 copy-start
  6.5 0.0 copy-start.5
  6.5 0.0 copy-start.3
  6.5 3.1 %slice.58 = f32[8,1,256,256]{3,2,1,0:T(8,128)} slice(f32[16,1,256,256]{3,2,1,0:T(8,128)} %param.5), slice={[0:8], [0:1], [0:256], [0:256]} | slice | bytes 4194304 | tf_op jit(solution)/shard_map/slice | solution.py:33
  9.7 11.6 %all-to-all-start = ((f32[32,64,256]{2,1,0:T(8,128)}), f32[32,64,256]{2,1,0:T(8,128)S(1)}, u32[]{:S(2)}, u32[]{:S(2)}) async-start(f32[32,64,256]{2,1,0:T(8,128)} %bitcast.2), calls=%async_computation | async-start | bytes 4194304 | tf_op jit(solution)/shard_map/all_to_all | solution.py:36
  21.3 0.0 copy-done.5
  21.3 0.7 fusion.24
  22.0 0.0 copy-done
  22.0 0.0 copy-done.3
  22.0 0.4 fusion.13
  22.4 48.1 %all-to-all-done = f32[32,64,256]{2,1,0:T(8,128)S(1)} async-done(((f32[32,64,256]{2,1,0:T(8,128)}), f32[32,64,256]{2,1,0:T(8,128)S(1)}, u32[]{:S(2)}, u32[]{:S(2)}) %all-to-all-start) | async-done | bytes 2097184 | tf_op jit(solution)/shard_map/all_to_all | solution.py:36
  70.5 0.9 convolution_select_fusion.1
  71.4 0.4 convolution_subtract_fusion
  71.8 1.1 fusion.7
  72.9 2.5 stack.11
  75.4 0.0 copy-start.4
  75.4 7.0 %all-to-all-start.1 = ((f32[32,2,64,256]{3,2,1,0:T(8,128)}), f32[32,2,64,256]{3,2,1,0:T(8,128)}, u32[]{:S(2)}, u32[]{:S(2)}) async-start(f32[32,2,64,256]{3,2,1,0:T(8,128)} %stack.11), calls=%async_computation.1 | async-start | bytes 8388608 | tf_op jit(solution)/shard_map/all_to_all | solution.py:13
  82.5 0.2 all-reduce.2.cloned.1.call-start
  82.7 0.0 copy-done.4
  82.8 91.5 %all-to-all-done.1 = f32[32,2,64,256]{3,2,1,0:T(8,128)} async-done(((f32[32,2,64,256]{3,2,1,0:T(8,128)}), f32[32,2,64,256]{3,2,1,0:T(8,128)}, u32[]{:S(2)}, u32[]{:S(2)}) %all-to-all-start.1) | async-done | bytes 4194336 | tf_op jit(solution)/shard_map/all_to_all | solution.py:13
  174.3 2.5 copy.12
  176.8 0.0 copy-start.2
  176.8 2.0 copy-done.2
  178.8 1.1 dynamic-slice_select_fusion
  179.9 0.0 all-reduce.2.cloned.1.call-update
  179.9 4.0 %fusion.22 = (f32[1,32,64,256]{3,2,1,0:T(8,128)S(1)}, f32[1,32,64,256]{3,2,1,0:T(8,128)}) fusion(f32[2,32,64,256]{3,2,1,0:T(8,128)} %bitcast.64), kind=kLoop, calls=%fused_computation.46 | loop fusion | bytes 8388608 | tf_op jit(solution)/shard_map/slice | solution.py:49
  183.9 2.8 gather_fusion
  186.7 4.4 %gather_fusion.1 = f32[16,256,256]{2,1,0:T(8,128)} fusion(f32[8,256,256]{2,1,0:T(8,128)} %bitcast.61, s32[1024]{0:T(1024)S(1)} %get-tuple-element.20), kind=kCustom, calls=%fused_computation.1 | custom fusion | bytes 8388672 | tf_op jit(solution)/shard_map/gather | solution.py:63
  191.1 56.5 %all-reduce.2.cloned.1.call-done = f32[2,2,256,256]{3,2,1,0:T(8,128)} async-done(((f32[2,2,256,256]{3,2,1,0:T(8,128)}), f32[2,2,256,256]{3,2,1,0:T(8,128)}) %all-reduce.2.cloned.1.call-update) | async-done | bytes 1048592 | tf_op jit(solution)/shard_map/psum | solution.py:19
  247.5 1.3 slice_bitcast_fusion.1
  248.8 2.8 gather_fusion.2
  251.6 2.8 gather_fusion.3
  254.4 0.0 copy-start.1
  254.4 22.4 %bitcast_subtract_fusion = f32[16,256,256]{2,1,0:T(8,128)S(1)} fusion(f32[16,1,256,256]{3,2,1,0:T(8,128)} %param.5, pred[16]{0:T(512)(128)(4,1)S(1)} %compare_bitcast_fusion, f32[16,256,256]{2,1,0:T(8,128)} %gather_fusion.3, f32[16,256,256]{2,1,0:T(8,128)} %gather_fusion.2, f32[16,256,256]{2,1,0:T(8,128)} %gather_fusion.1, f32[16,256,256]{2,1,0:T(8,128)} %gather_fusion), kind=kOutput, calls=%fused_computation.12 | convolution fusion | flops 6448742400 | bytes 25165840 | tf_op jit(solution)/shard_map/sak,sbk->sab/dot_general | solution.py:65
  276.9 0.0 copy-done.1
  276.9 0.6 slice_select_fusion
  277.5 2.4 maximum_bitcast_fusion
  (7 shorter events, 0.0 us)
Async XLA Ops:
  6.5 15.5 %copy-start = (f32[256,256]{1,0:T(8,128)S(1)}, f32[256,256]{1,0:T(8,128)}, u32[]{:S(2)}) copy-start(f32[256,256]{1,0:T(8,128)} %param.9) | copy-start | bytes 786436
  6.5 14.8 %copy-start.5 = (s32[2,8]{1,0:T(2,128)S(1)}, s32[2,8]{1,0:T(2,128)}, u32[]{:S(2)}) copy-start(s32[2,8]{1,0:T(2,128)} %param.6) | copy-start | bytes 196
  6.5 15.5 %copy-start.3 = (f32[2,256,256]{2,1,0:T(8,128)S(1)}, f32[2,256,256]{2,1,0:T(8,128)}, u32[]{:S(2)}) copy-start(f32[2,256,256]{2,1,0:T(8,128)} %param.8) | copy-start | bytes 1572868
  9.7 60.9 %all-to-all-start = ((f32[32,64,256]{2,1,0:T(8,128)}), f32[32,64,256]{2,1,0:T(8,128)S(1)}, u32[]{:S(2)}, u32[]{:S(2)}) async-start(f32[32,64,256]{2,1,0:T(8,128)} %bitcast.2), calls=%async_computation | async-start | bytes 4194304 | tf_op jit(solution)/shard_map/all_to_all | solution.py:36
  75.4 7.3 %copy-start.4 = (s32[2,16,1]{1,2,0:T(1,128)S(1)}, s32[2,16,1]{1,2,0:T(1,128)}, u32[]{:S(2)}) copy-start(s32[2,16,1]{1,2,0:T(1,128)} %param.7) | copy-start | bytes 388
  75.4 98.9 %all-to-all-start.1 = ((f32[32,2,64,256]{3,2,1,0:T(8,128)}), f32[32,2,64,256]{3,2,1,0:T(8,128)}, u32[]{:S(2)}, u32[]{:S(2)}) async-start(f32[32,2,64,256]{3,2,1,0:T(8,128)} %stack.11), calls=%async_computation.1 | async-start | bytes 8388608 | tf_op jit(solution)/shard_map/all_to_all | solution.py:13
  82.5 165.1 %all-reduce.2.cloned.1.call-start = ((), (), s32[]{:S(2)}) async-start(), calls=%async_computation.2 | async-start | bytes 2097152 | tf_op jit(solution)/shard_map/psum | solution.py:19
  176.8 2.0 copy-start.2
  254.4 22.5 %copy-start.1 = (f32[1,32,64,256]{3,2,1,0:T(8,128)S(1)}, f32[1,32,64,256]{3,2,1,0:T(8,128)}, u32[]{:S(2)}) copy-start(f32[1,32,64,256]{3,2,1,0:T(8,128)} %get-tuple-element.8) | copy-start | bytes 6291460
Sparse Core Ops, SparseCore 0:
  180.0 67.4 all-reduce.1
